TPU v7x, 512 devices: a whole 4x4x16 slice. The times are simulated.
512 devices in a mesh: row: 32 (over x, y, core), col: 16 (over z).
Axes of the slice: x: 4, y: 4, z: 16, core: 2. Of those that a mesh axis runs over, the one named last changes fastest.
Arguments:
- panel: float32 [65536, 256], P('row', 'col'), may hold values from -210 to 210
- slab: float32 [65536, 4096], P('row', 'col'), may hold values from -6 to 6
Outputs:
- triangle: float32 [256, 256], P(None, 'col')
- projected: float32 [256, 4096], P(None, 'col')
- residual: float32 [65536, 4096], P('row', 'col')
All inputs are finite; a program needn't handle non-finite values.
Results may differ from a plain program's by a relative error of at most 0.0003.
Values sent between devices are 32-bit elements; how exact they have to be, the bound alone decides.
No kernel may reach another device: no remote copies, remote signals or barrier semaphores. Data moves between devices by JAX's collectives and lax.ppermute only.
A program may use at most 64 MiB of HBM per device.

v0:
```python
import math
import jax
import jax.numpy as jnp
from jax import lax
from jax.sharding import PartitionSpec as P

contract_rows = (((0,), (0,)), ((), ()))


def row_sum(x):
    n = lax.axis_size("row")
    rows, cols = x.shape
    parts = x.reshape(n, rows // n, cols)
    mine = lax.all_to_all(parts, "row", 0, 0, tiled=False).sum(0)
    copies = jnp.broadcast_to(mine[None], (n, rows // n, cols))
    return lax.all_to_all(copies, "row", 0, 0, tiled=False).reshape(rows, cols)


def per_device(panel, slab):
    highest = lax.Precision.HIGHEST
    gathered = lax.all_gather(panel, "col", axis=1, tiled=True)
    cross_local = lax.dot_general(gathered, slab, contract_rows, precision=highest)
    gram_local = lax.dot_general(gathered, gathered, contract_rows, precision=highest)
    width = gram_local.shape[1]
    summed = row_sum(jnp.concatenate([gram_local, cross_local], axis=1))
    gram_total, totals = (summed[:, :width], summed[:, width:])
    lower_factor = jnp.linalg.cholesky(gram_total)
    projected = lax.linalg.triangular_solve(
        lower_factor, totals, left_side=True, lower=True, transpose_a=False
    )
    coefficients = lax.linalg.triangular_solve(
        lower_factor, projected, left_side=True, lower=True, transpose_a=True
    )
    residual = slab - jnp.dot(gathered, coefficients, precision=highest)
    col_width = panel.shape[1]
    rows_total = gathered.shape[0] * lax.axis_size("row")
    scaled = lower_factor.T * (1.0 / math.sqrt(rows_total))
    triangle = lax.dynamic_slice_in_dim(scaled, lax.axis_index("col") * col_width, col_width, 1)
    return (triangle, projected, residual)


def solution(mesh):
    placed = (P("row", "col"), P("row", "col"))
    return jax.shard_map(
        per_device,
        mesh=mesh,
        in_specs=placed,
        out_specs=(P(None, "col"), P(None, "col"), P("row", "col")),
        check_vma=False,
    )
```

profile of v0, /device:TPU:1, one launch (start us, length us, event | category | flops | bytes accessed | tf_op | source)
XLA Modules:
  0.0 207.8 jit_solution(18180346574200016031)
XLA Ops:
  7.2 0.0 all-gather.2.cloned.1.call-start
  7.2 0.7 all-gather.2.cloned.1.call-update
  7.9 71.6 %all-gather.2.cloned.1.call-done = f32[2048,256]{0,1:T(8,128)} async-done(((f32[2048,16]{0,1:T(8,128)}), f32[2048,256]{0,1:T(8,128)}) %all-gather.2.cloned.1.call-update) | async-done | bytes 2097168 | tf_op jit(solution)/shard_map/all_gather | solution.py:21
  79.5 0.0 copy-start
  79.5 0.0 copy-start.2
  79.5 4.2 %fusion.19 = f32[256,256]{0,1:T(8,128)S(1)} fusion(f32[2048,256]{0,1:T(8,128)} %all-gather.2.cloned.1.call-done), kind=kOutput, calls=%fused_computation.43 | convolution fusion | flops 1610612736 | bytes 2359296 | tf_op jit(solution)/shard_map/dot_general | solution.py:23
  83.7 0.0 copy-done
  83.7 0.0 copy-done.2
  83.7 3.6 %fusion.20 = f32[256,256]{0,1:T(8,128)S(1)} fusion(f32[2048,256]{0,1:T(8,128)S(1)} %copy-done, f32[2048,256]{1,0:T(8,128)S(1)} %copy-done.2), kind=kOutput, calls=%fused_computation.44 | convolution fusion | flops 1610612736 | bytes 4456448 | tf_op jit(solution)/shard_map/dot_general | solution.py:22
  87.3 0.2 copy.8
  87.5 28.0 %all_to_all.10 = f32[32,8,512]{2,1,0:T(8,128)S(1)} all-to-all(f32[32,8,512]{2,1,0:T(8,128)S(1)} %bitcast.53), channel_id=1, replica_groups=mesh['row'=32,'col'=16] {'row'}, dimensions={0} | all-to-all | bytes 1048576 | tf_op jit(solution)/shard_map/all_to_all | solution.py:14
  115.6 0.8 broadcast_in_dim.3
  116.4 3.9 %all-to-all-start.1 = ((f32[32,8,512]{2,1,0:T(8,128)}), f32[32,8,512]{2,1,0:T(8,128)S(1)}, u32[]{:S(2)}, u32[]{:S(2)}) async-start(f32[32,8,512]{2,1,0:T(8,128)} %broadcast_in_dim.3), calls=%async_computation.1 | async-start | bytes 1048576 | tf_op jit(solution)/shard_map/all_to_all | solution.py:16
  120.3 2.9 %copy.11 = f32[2048,256]{0,1:T(8,128)} copy(f32[2048,256]{1,0:T(8,128)} %param.3) | data formatting | bytes 4194304 | tf_op args[1]
  123.2 8.5 %all-to-all-done.1 = f32[32,8,512]{2,1,0:T(8,128)S(1)} async-done(((f32[32,8,512]{2,1,0:T(8,128)}), f32[32,8,512]{2,1,0:T(8,128)S(1)}, u32[]{:S(2)}, u32[]{:S(2)}) %all-to-all-start.1) | async-done | bytes 524320 | tf_op jit(solution)/shard_map/all_to_all | solution.py:16
  131.7 0.1 copy.13
  131.9 11.7 %cholesky.50 = f32[128,128]{1,0:T(8,128)S(1)} custom-call(f32[128,128]{1,0:T(8,128)S(1)} %cholesky.118), custom_call_target="Cholesky" | custom-call | tf_op jit(solution)/shard_map/jit(cholesky)/cholesky | solution.py:27
  143.7 9.8 %custom-call.16 = f32[1,128,128]{1,2,0:T(8,128)S(1)} custom-call(f32[1,128,128]{2,1,0:T(8,128)S(1)} %get-tuple-element.32), custom_call_target="InvertDiagBlocksLowerTriangular" | custom-call | tf_op jit(solution)/shard_map/jit(cholesky)/cholesky | solution.py:27
  153.5 0.2 constant_dynamic-update-slice_fusion
  153.7 0.3 convolution_subtract_fusion.2
  154.0 11.7 %cholesky.105 = f32[128,128]{1,0:T(8,128)S(1)} custom-call(f32[128,128]{1,0:T(8,128)S(1)} %convolution_subtract_fusion.2), custom_call_target="Cholesky" | custom-call | tf_op jit(solution)/shard_map/jit(cholesky)/cholesky | solution.py:27
  165.7 0.6 compare_reduce_fusion
  167.7 0.1 triangular_solve.53
  167.8 4.0 %while.1 = (s32[]{:T(128)}, f32[256,256]{1,0:T(8,128)S(1)}, s32[2,2]{1,0:T(2,128)S(1)}, f32[2,128,128]{2,1,0:T(8,128)S(1)}, s32[]{:T(128)}) while((s32[]{:T(128)}, f32[256,256]{1,0:T(8,128)S(1)}, s32[2,2]{1,0:T(2,128)S(1)}, f32[2,128,128]{2,1,0:T(8,128)S(1)}, s32[]{:T(128)}) %tuple.30), condition=%wide.while_cond, body=%wide.while_body.sunk | while | flops 2 | bytes 131189 | solution.py:28
  167.8 0.6 fusion.34
  168.4 1.4 bitcast_dynamic-update-slice_fusion.2
  169.8 0.6 fusion.34
  170.4 1.4 bitcast_dynamic-update-slice_fusion.2
  171.8 19.9 %custom-call.17 = f32[2,128,128]{1,2,0:T(8,128)S(1)} custom-call(f32[2,128,128]{2,1,0:T(8,128)S(1)} %get-tuple-element.10), custom_call_target="InvertDiagBlocksLowerTriangular" | custom-call | tf_op jit(solution)/shard_map/triangular_solve | solution.py:28
  191.7 0.0 copy-start.1
  191.7 0.3 fusion.6
  192.0 0.3 convolution_subtract_fusion.1
  192.3 0.3 fusion.13
  192.6 0.3 fusion.12
  192.9 0.7 pad_maximum_fusion.1
  193.6 0.3 convolution_subtract_fusion
  193.9 0.3 fusion.11
  194.2 0.0 copy-done.1
  194.2 3.3 %fusion = f32[2048,256]{0,1:T(8,128)} fusion(f32[2048,256]{0,1:T(8,128)S(1)} %copy-done.1, f32[2048,256]{0,1:T(8,128)S(1)} %copy-done, f32[128,256]{1,0:T(8,128)S(1)} %fusion.12, f32[128,256]{1,0:T(8,128)S(1)} %fusion.11), kind=kOutput, calls=%fused_computation.3 | convolution fusion | flops 1611202560 | bytes 6553600 | tf_op jit(solution)/shard_map/dot_general | solution.py:34
  197.5 2.9 %copy.12 = f32[2048,256]{1,0:T(8,128)} copy(f32[2048,256]{0,1:T(8,128)} %fusion) | data formatting | bytes 4194304
  200.4 0.6 fusion.16
  (13 shorter events, 0.3 us)
Async XLA Ops:
  7.2 72.3 %all-gather.2.cloned.1.call-start = ((), (), s32[]{:S(2)}) async-start(), calls=%async_computation.2 | async-start | bytes 2228224 | tf_op jit(solution)/shard_map/all_gather | solution.py:21
  79.5 4.2 %copy-start = (f32[2048,256]{0,1:T(8,128)S(1)}, f32[2048,256]{0,1:T(8,128)}, u32[]{:S(2)}) copy-start(f32[2048,256]{0,1:T(8,128)} %all-gather.2.cloned.1.call-done) | copy-start | bytes 6291460
  79.5 4.2 %copy-start.2 = (f32[2048,256]{1,0:T(8,128)S(1)}, f32[2048,256]{1,0:T(8,128)}, u32[]{:S(2)}) copy-start(f32[2048,256]{1,0:T(8,128)} %param.3) | copy-start | bytes 6291460
  116.4 15.3 %all-to-all-start.1 = ((f32[32,8,512]{2,1,0:T(8,128)}), f32[32,8,512]{2,1,0:T(8,128)S(1)}, u32[]{:S(2)}, u32[]{:S(2)}) async-start(f32[32,8,512]{2,1,0:T(8,128)} %broadcast_in_dim.3), calls=%async_computation.1 | async-start | bytes 1048576 | tf_op jit(solution)/shard_map/all_to_all | solution.py:16
  191.7 2.5 %copy-start.1 = (f32[2048,256]{0,1:T(8,128)S(1)}, f32[2048,256]{0,1:T(8,128)}, u32[]{:S(2)}) copy-start(f32[2048,256]{0,1:T(8,128)} %copy.11) | copy-start | bytes 6291460
Sparse Core Ops, SparseCore 0:
  10.1 69.3 all-gather.1
where the time goes:
time: 208 us
  waiting for transfers between devices  80.7 us (39%)
  other arithmetic  55.3 us (27%)
  blocking collectives  28 us (13%)
  between operations  15.5 us (7%)
  matrix products  13.3 us (6%)
  local copies, waits for them, and re-layouts  11 us (5%)
  starting transfers between devices  3.89 us (2%)
    all_gather x1, waiting for transfers between devices, per_device(): gathered = lax.all_gather(panel, 'col', axis=1, tiled=True)  71.6 us
    another operation x6, other arithmetic, per_device(): lower_factor = jnp.linalg.cholesky(gram_total)  33.9 us
    all_to_all x1, blocking collectives, row_sum(): mine = lax.all_to_all(parts, 'row', 0, 0, tiled=False).sum(0)  28 us
    another operation x4, other arithmetic, per_device(): lax.linalg.triangular_solve(lower_factor, totals, left_side=True, lower=T...  20.7 us
    all_to_all x1, waiting for transfers between devices, row_sum(): return lax.all_to_all(copies, 'row', 0, 0, tiled=False).reshape(rows, cols)  8.49 us
    unnamed x9, local copies, waits for them, and re-layouts  5.91 us
    dot_general x1, matrix products, per_device(): lax.dot_general(gathered, gathered, contract_rows, precision=highest)  4.23 us
  transfers between devices with their start and end apart: 2, of which 2 were waited for; matrix products, arithmetic and copies ran while one was open for 1% of the time, Pallas kernels for 0%

commit v1 on v0

--- a/solution.py
+++ b/solution.py
@@ -18,7 +18,9 @@
 
 def per_device(panel, slab):
     highest = lax.Precision.HIGHEST
-    gathered = lax.all_gather(panel, "col", axis=1, tiled=True)
+    gathered = jnp.concatenate(
+        lax.all_to_all(jnp.stack([panel] * lax.axis_size("col")), "col", 0, 0), axis=1
+    )
     cross_local = lax.dot_general(gathered, slab, contract_rows, precision=highest)
     gram_local = lax.dot_general(gathered, gathered, contract_rows, precision=highest)
     width = gram_local.shape[1]

time: 208 us -> 225 us (1.082)
  blocking collectives: 28 us -> 132 us
  waiting for transfers between devices: 80.7 us -> 8.49 us
  between operations: 15.5 us -> 2.14 us
  matrix products: 13.3 us -> 10.9 us
    all_to_all x0 -> x1, blocking collectives: none -> 106 us  [per_device(): lax.all_to_all(jnp.stack([panel] * lax.axis_size('col')), 'col', 0, 0)]
    all_gather x1 -> x0, waiting for transfers between devices: 71.6 us -> none  [per_device(): gathered = lax.all_gather(panel, 'col', axis=1, tiled=True)]
    dot_general x1, matrix products: 4.23 us -> 1.86 us  [per_device(): lax.dot_general(gathered, gathered, contract_rows, precision=highest)]
    all_to_all x1, blocking collectives: 28 us -> 25.7 us  [row_sum(): mine = lax.all_to_all(parts, 'row', 0, 0, tiled=False).sum(0)]
    another operation x6 -> x7, local copies, waits for them, and re-layouts: 3.95 us -> 5.09 us
    unnamed x9 -> x7, local copies, waits for them, and re-layouts: 5.91 us -> 5.9 us
  transfers between devices with their start and end apart: 2 -> 1, of which waited for: 2 -> 1; matrix products, arithmetic and copies ran while one was open for 1% -> 1% of each run, Pallas kernels for 0% -> 0%
where the time goes in v1:
time: 225 us; the launch traced here: 224 us
  blocking collectives  132 us (59%)
  other arithmetic  55.3 us (25%)
  local copies, waits for them, and re-layouts  12.1 us (5%)
  matrix products  10.9 us (5%)
  waiting for transfers between devices  8.49 us (4%)
  starting transfers between devices  3.85 us (2%)
    all_to_all x1, blocking collectives, per_device(): lax.all_to_all(jnp.stack([panel] * lax.axis_size('col')), 'col', 0, 0)  106 us
    another operation x6, other arithmetic, per_device(): lower_factor = jnp.linalg.cholesky(gram_total)  33.9 us
    all_to_all x1, blocking collectives, row_sum(): mine = lax.all_to_all(parts, 'row', 0, 0, tiled=False).sum(0)  25.7 us
    another operation x4, other arithmetic, per_device(): lax.linalg.triangular_solve(lower_factor, totals, left_side=True, lower=T...  20.7 us
    all_to_all x1, waiting for transfers between devices, row_sum(): return lax.all_to_all(copies, 'row', 0, 0, tiled=False).reshape(rows, cols)  8.49 us
    unnamed x7, local copies, waits for them, and re-layouts  5.9 us
  transfers between devices with their start and end apart: 1, of which 1 were waited for; matrix products, arithmetic and copies ran while one was open for 1% of the time, Pallas kernels for 0%

profile of v1, /device:TPU:1, one launch (start us, length us, event | category | flops | bytes accessed | tf_op | source)
XLA Modules:
  0.0 224.5 jit_solution(6646721721641392971)
XLA Ops:
  0.6 1.1 stack.2
  1.8 105.8 %all_to_all.15 = f32[16,2048,16]{1,2,0:T(8,128)S(1)} all-to-all(f32[16,2048,16]{1,2,0:T(8,128)S(1)} %stack.2), channel_id=1, replica_groups=mesh['row'=32,'col'=16] {'col'}, dimensions={0} | all-to-all | bytes 4194304 | tf_op jit(solution)/shard_map/all_to_all | solution.py:22
  107.6 0.0 copy-start.1
  107.6 1.9 fusion.19
  109.4 0.0 copy-done.1
  109.4 3.6 %fusion.20 = f32[256,256]{0,1:T(8,128)S(1)} fusion(f32[2048,256]{0,1:T(8,128)S(1)} %bitcast.53, f32[2048,256]{1,0:T(8,128)S(1)} %copy-done.1), kind=kOutput, calls=%fused_computation.44 | convolution fusion | flops 1610612736 | bytes 4456448 | tf_op jit(solution)/shard_map/dot_general | solution.py:24
  113.1 0.2 copy.9
  113.3 25.7 %all_to_all.16 = f32[32,8,512]{2,1,0:T(8,128)S(1)} all-to-all(f32[32,8,512]{2,1,0:T(8,128)S(1)} %bitcast.59), channel_id=1, replica_groups=mesh['row'=32,'col'=16] {'row'}, dimensions={0} | all-to-all | bytes 1048576 | tf_op jit(solution)/shard_map/all_to_all | solution.py:14
  139.0 0.9 broadcast_in_dim.3
  139.9 3.9 %all-to-all-start.2 = ((f32[32,8,512]{2,1,0:T(8,128)}), f32[32,8,512]{2,1,0:T(8,128)S(1)}, u32[]{:S(2)}, u32[]{:S(2)}) async-start(f32[32,8,512]{2,1,0:T(8,128)} %broadcast_in_dim.3), calls=%async_computation.2 | async-start | bytes 1048576 | tf_op jit(solution)/shard_map/all_to_all | solution.py:16
  143.7 2.9 %copy.12 = f32[2048,256]{0,1:T(8,128)} copy(f32[2048,256]{1,0:T(8,128)} %param.3) | data formatting | bytes 4194304 | tf_op args[1]
  146.6 8.5 %all-to-all-done.2 = f32[32,8,512]{2,1,0:T(8,128)S(1)} async-done(((f32[32,8,512]{2,1,0:T(8,128)}), f32[32,8,512]{2,1,0:T(8,128)S(1)}, u32[]{:S(2)}, u32[]{:S(2)}) %all-to-all-start.2) | async-done | bytes 524320 | tf_op jit(solution)/shard_map/all_to_all | solution.py:16
  155.1 0.1 copy.14
  155.3 11.7 %cholesky.50 = f32[128,128]{1,0:T(8,128)S(1)} custom-call(f32[128,128]{1,0:T(8,128)S(1)} %cholesky.118), custom_call_target="Cholesky" | custom-call | tf_op jit(solution)/shard_map/jit(cholesky)/cholesky | solution.py:29
  167.1 9.8 %custom-call.16 = f32[1,128,128]{1,2,0:T(8,128)S(1)} custom-call(f32[1,128,128]{2,1,0:T(8,128)S(1)} %get-tuple-element.32), custom_call_target="InvertDiagBlocksLowerTriangular" | custom-call | tf_op jit(solution)/shard_map/jit(cholesky)/cholesky | solution.py:29
  176.9 0.2 constant_dynamic-update-slice_fusion
  177.1 0.3 convolution_subtract_fusion.2
  177.4 11.7 %cholesky.105 = f32[128,128]{1,0:T(8,128)S(1)} custom-call(f32[128,128]{1,0:T(8,128)S(1)} %convolution_subtract_fusion.2), custom_call_target="Cholesky" | custom-call | tf_op jit(solution)/shard_map/jit(cholesky)/cholesky | solution.py:29
  189.2 0.6 compare_reduce_fusion
  191.2 0.1 triangular_solve.53
  191.2 4.0 %while.1 = (s32[]{:T(128)}, f32[256,256]{1,0:T(8,128)S(1)}, s32[2,2]{1,0:T(2,128)S(1)}, f32[2,128,128]{2,1,0:T(8,128)S(1)}, s32[]{:T(128)}) while((s32[]{:T(128)}, f32[256,256]{1,0:T(8,128)S(1)}, s32[2,2]{1,0:T(2,128)S(1)}, f32[2,128,128]{2,1,0:T(8,128)S(1)}, s32[]{:T(128)}) %tuple.30), condition=%wide.while_cond, body=%wide.while_body.sunk | while | flops 2 | bytes 131189 | solution.py:30
  191.2 0.6 fusion.34
  191.8 1.4 bitcast_dynamic-update-slice_fusion.2
  193.2 0.6 fusion.34
  193.8 1.4 bitcast_dynamic-update-slice_fusion.2
  195.2 19.9 %custom-call.17 = f32[2,128,128]{1,2,0:T(8,128)S(1)} custom-call(f32[2,128,128]{2,1,0:T(8,128)S(1)} %get-tuple-element.10), custom_call_target="InvertDiagBlocksLowerTriangular" | custom-call | tf_op jit(solution)/shard_map/triangular_solve | solution.py:30
  215.1 0.0 copy-start
  215.1 0.3 fusion.6
  215.5 0.3 convolution_subtract_fusion.1
  215.7 0.3 fusion.13
  216.0 0.3 fusion.12
  216.3 0.7 pad_maximum_fusion.1
  217.0 0.3 convolution_subtract_fusion
  217.3 0.3 fusion.11
  217.6 0.0 copy-done
  217.6 3.3 %fusion = f32[2048,256]{0,1:T(8,128)} fusion(f32[2048,256]{0,1:T(8,128)S(1)} %copy-done, f32[2048,256]{0,1:T(8,128)S(1)} %bitcast.54, f32[128,256]{1,0:T(8,128)S(1)} %fusion.12, f32[128,256]{1,0:T(8,128)S(1)} %fusion.11), kind=kOutput, calls=%fused_computation.3 | convolution fusion | flops 1611202560 | bytes 6553600 | tf_op jit(solution)/shard_map/dot_general | solution.py:36
  221.0 2.9 %copy.13 = f32[2048,256]{1,0:T(8,128)} copy(f32[2048,256]{0,1:T(8,128)} %fusion) | data formatting | bytes 4194304
  223.9 0.6 fusion.16
  (13 shorter events, 0.3 us)
Async XLA Ops:
  107.6 1.9 copy-start.1
  139.9 15.3 %all-to-all-start.2 = ((f32[32,8,512]{2,1,0:T(8,128)}), f32[32,8,512]{2,1,0:T(8,128)S(1)}, u32[]{:S(2)}, u32[]{:S(2)}) async-start(f32[32,8,512]{2,1,0:T(8,128)} %broadcast_in_dim.3), calls=%async_computation.2 | async-start | bytes 1048576 | tf_op jit(solution)/shard_map/all_to_all | solution.py:16
  215.1 2.5 %copy-start = (f32[2048,256]{0,1:T(8,128)S(1)}, f32[2048,256]{0,1:T(8,128)}, u32[]{:S(2)}) copy-start(f32[2048,256]{0,1:T(8,128)} %copy.12) | copy-start | bytes 6291460
